TPU v7x, 32 devices: a whole 2x2x4 slice. The times are simulated.
32 devices in a mesh: groups: 2 (over y), pairs: 4 (over z), mp: 4 (over x, core).
Axes of the slice: x: 2, y: 2, z: 4, core: 2. Of those that a mesh axis runs over, the one named last changes fastest.
Arguments:
- tokens: bfloat16 [512, 768], P(('groups', 'pairs'), 'mp'), parts along dimension 0, may hold values from -6 to 6
- pair_list: int32 [16, 2], P(('groups', 'pairs')), parts along dimension 0, may hold values from 0 to 7, as said below
- confidence: float32 [16, 64], P(('groups', 'pairs')), parts along dimension 0, may hold values from 0.1 to 10
- gain_self: float32 [768], replicated, may hold values from 0.1 to 1.9
- gain_query: float32 [768], replicated, may hold values from 0.1 to 1.9
- gain_context: float32 [768], replicated, may hold values from 0.1 to 1.9
- gain_mlp: float32 [768], replicated, may hold values from 0.1 to 1.9
- self_qkv: bfloat16 [3, 768, 768], P(None, None, 'mp'), may hold values from -1 to 1
- self_out: bfloat16 [768, 768], P('mp'), may hold values from -0.21875 to 0.21875
- cross_query: bfloat16 [768, 768], P(None, 'mp'), may hold values from -1 to 1
- cross_kv: bfloat16 [2, 768, 768], P(None, None, 'mp'), may hold values from -1 to 1
- cross_out: bfloat16 [768, 768], P('mp'), may hold values from -0.21875 to 0.21875
- mlp_up: bfloat16 [768, 3072], P(None, 'mp'), may hold values from -0.21875 to 0.21875
- mlp_down: bfloat16 [3072, 768], P('mp'), may hold values from -0.109375 to 0.109375
Outputs:
- image_features: bfloat16 [512, 768], P(('groups', 'pairs'), 'mp'), parts along dimension 0
There are 2 independent parts, one for each index of `groups`. A program takes and returns all parts, laid end to end along the dimension named above; an argument that names none is the same for every part. Nothing has to cross between parts.
Inputs may be any that keep to these rules, and one draw needn't show every extreme that they name: `pair_list`: in each block of 2 consecutive pairs the 4 images named are distinct and have distinct owners, the owner of image i being i // 2; the images of each owner are named in exactly 4 blocks; some images are named by no pair.
All inputs are finite; a program needn't handle non-finite values.
Results may differ from a plain program's by a relative error of at most 0.012.
Values may be sent and summed in bfloat16 or wider, within the bound.
No kernel may reach another device: no remote copies, remote signals or barrier semaphores. Data moves between devices by JAX's collectives and lax.ppermute only.
A program may use at most 64 MiB of HBM per device.

v0:
```python
import jax
import jax.numpy as jnp
from jax import lax
from jax.sharding import PartitionSpec as P

HEAD = 64
TOKS = 32
EPSILON = 1e-06


def layer_norm(values, gain):
    center = values - jnp.mean(values, axis=-1, keepdims=True)
    spread = jnp.mean(center * center, axis=-1, keepdims=True)
    return (center * lax.rsqrt(spread + EPSILON) * gain).astype(jnp.bfloat16)


def attend(query, keys, values, views_n):
    rows_n, width = query.shape
    heads_n = width // HEAD
    qh = query.reshape(views_n, TOKS, heads_n, HEAD)
    kh = keys.reshape(views_n, TOKS, heads_n, HEAD)
    vh = values.reshape(views_n, TOKS, heads_n, HEAD)
    scores = jnp.einsum("vqhc,vkhc->vhqk", qh, kh, preferred_element_type=jnp.float32) * HEAD ** (
        -0.5
    )
    probs = jax.nn.softmax(scores, axis=-1).astype(jnp.bfloat16)
    mixed = jnp.einsum("vhqk,vkhc->vqhc", probs, vh, preferred_element_type=jnp.float32)
    return mixed.astype(jnp.bfloat16).reshape(rows_n, width)


def partner(values):
    shape = values.shape
    paired = values.reshape((shape[0] // 2, 2) + shape[1:])
    return jnp.flip(paired, axis=1).reshape(shape)


def summed_full(term):
    return lax.psum(term.astype(jnp.bfloat16), "mp").astype(jnp.float32)


def per_device(
    tokens,
    pair_list,
    confidence,
    gain_self,
    gain_query,
    gain_context,
    gain_mlp,
    self_qkv,
    self_out,
    cross_query,
    cross_kv,
    cross_out,
    mlp_up,
    mlp_down,
):
    quarter = tokens.shape[1]
    img_dev = tokens.shape[0] // TOKS
    pair_dev = pair_list.shape[0]
    views_n = 2 * pair_dev
    owners_n = lax.axis_size("pairs")
    own = lax.axis_index("pairs")
    table = lax.all_gather(pair_list, "pairs", axis=0, tiled=True).reshape(owners_n, views_n)
    wanted = jnp.where(table // img_dev == own, table % img_dev, -1)
    chosen = jnp.max(wanted, axis=1)
    images = tokens.reshape(img_dev, TOKS, quarter)
    picked = jnp.take(images, jnp.maximum(chosen, 0), axis=0)
    outgoing = jnp.where((chosen >= 0)[:, None, None], picked, jnp.zeros_like(picked))
    arrived = lax.all_to_all(outgoing, "pairs", split_axis=0, concat_axis=0, tiled=True)
    source = pair_list.reshape(views_n) // img_dev
    slices = jnp.take(arrived, source, axis=0)
    start = lax.all_gather(slices, "mp", axis=2, tiled=True)
    width = start.shape[2]
    rows_n = views_n * TOKS
    begin = start.astype(jnp.float32).reshape(rows_n, width)
    context = layer_norm(partner(start.astype(jnp.float32)), gain_context).reshape(rows_n, width)
    offset = lax.axis_index("mp") * quarter
    normed = layer_norm(begin, gain_self)
    qkv = jnp.einsum("rd,kdc->krc", normed, self_qkv, preferred_element_type=jnp.float32).astype(
        jnp.bfloat16
    )
    term = jnp.dot(
        attend(qkv[0], qkv[1], qkv[2], views_n), self_out, preferred_element_type=jnp.float32
    )
    resid = begin + summed_full(term)
    normed = layer_norm(resid, gain_query)
    query = jnp.dot(normed, cross_query, preferred_element_type=jnp.float32).astype(jnp.bfloat16)
    keyval = jnp.einsum(
        "rd,kdc->krc", context, cross_kv, preferred_element_type=jnp.float32
    ).astype(jnp.bfloat16)
    term = jnp.dot(
        attend(query, keyval[0], keyval[1], views_n), cross_out, preferred_element_type=jnp.float32
    )
    resid = resid + summed_full(term)
    normed = layer_norm(resid, gain_mlp)
    hidden = jax.nn.gelu(
        jnp.dot(normed, mlp_up, preferred_element_type=jnp.float32), approximate=False
    )
    term = jnp.dot(hidden.astype(jnp.bfloat16), mlp_down, preferred_element_type=jnp.float32)
    resid = resid + summed_full(term)
    final = lax.dynamic_slice_in_dim(resid, offset, quarter, 1)
    conf = confidence.reshape(views_n, TOKS)
    weighted = (final.reshape(views_n, TOKS, quarter) * conf[:, :, None]).reshape(
        views_n, TOKS * quarter
    )
    route = (source[None, :] == jnp.arange(owners_n)[:, None]).astype(jnp.float32)
    back = jnp.dot(route, weighted, precision=lax.Precision.HIGHEST).astype(jnp.bfloat16)
    back_weight = jnp.dot(route, conf, precision=lax.Precision.HIGHEST).astype(jnp.bfloat16)
    got_feat, got_weight = (
        lax.all_to_all(
            back.reshape(owners_n, TOKS, quarter), "pairs", split_axis=0, concat_axis=0, tiled=True
        ),
        lax.all_to_all(back_weight, "pairs", split_axis=0, concat_axis=0, tiled=True),
    )
    owner_match = chosen[None, :] == jnp.arange(img_dev)[:, None]
    numer = jnp.einsum(
        "ij,jtc->itc",
        owner_match.astype(jnp.bfloat16),
        got_feat,
        preferred_element_type=jnp.float32,
    )
    denom = jnp.dot(
        owner_match.astype(jnp.float32),
        got_weight.astype(jnp.float32),
        precision=lax.Precision.HIGHEST,
    )
    result = numer / jnp.maximum(denom, 1.0)[:, :, None]
    return result.astype(jnp.bfloat16).reshape(img_dev * TOKS, quarter)


def solution(mesh):
    return jax.shard_map(
        per_device,
        mesh=mesh,
        in_specs=(
            P(("groups", "pairs"), "mp"),
            P(("groups", "pairs"), None),
            P(("groups", "pairs"), None),
            P(),
            P(),
            P(),
            P(),
            P(None, None, "mp"),
            P("mp", None),
            P(None, "mp"),
            P(None, None, "mp"),
            P("mp", None),
            P(None, "mp"),
            P("mp", None),
        ),
        out_specs=P(("groups", "pairs"), "mp"),
        check_vma=False,
    )
```

profile of v0, /device:TPU:0, one launch (start us, length us, event | category | flops | bytes accessed | tf_op | source)
XLA Modules:
  0.0 180.7 jit_solution(869110114710449456)
XLA Ops:
  6.5 13.0 %all-gather = s32[4,2,2]{2,1,0:T(2,128)S(1)} all-gather(s32[1,2,2]{2,1,0:T(2,128)} %bitcast.90), channel_id=1, replica_groups=mesh['groups'=2,'pairs'=4,'mp'=4] {'pairs'}, dimensions={0}, use_global_device_ids=true | all-gather | bytes 80 | tf_op jit(solution)/shard_map/all_gather | solution.py:63
  19.7 0.1 reduce_max.36
  19.9 0.5 copy-done.11
  20.4 1.3 gather_fusion
  21.7 0.7 select_select_fusion
  22.4 3.3 %all-to-all-start = ((bf16[4,32,192]{2,1,0:T(8,128)(2,1)}), bf16[4,32,192]{2,1,0:T(8,128)(2,1)S(1)}, u32[]{:S(2)}, u32[]{:S(2)}) async-start(bf16[4,32,192]{2,1,0:T(8,128)(2,1)} %select_select_fusion), calls=%async_computation | async-start | bytes 131072 | tf_op jit(solution)/shard_map/all_to_all | solution.py:69
  25.7 0.8 reshape.277
  26.5 0.8 reshape.275
  27.3 0.5 compare_and_fusion
  27.8 3.6 %all-to-all-done = bf16[4,32,192]{2,1,0:T(8,128)(2,1)S(1)} async-done(((bf16[4,32,192]{2,1,0:T(8,128)(2,1)}), bf16[4,32,192]{2,1,0:T(8,128)(2,1)S(1)}, u32[]{:S(2)}, u32[]{:S(2)}) %all-to-all-start) | async-done | bytes 49184 | tf_op jit(solution)/shard_map/all_to_all | solution.py:69
  31.4 0.5 gather_fusion.1
  32.0 0.2 copy.73
  32.2 8.6 %all_gather.7 = bf16[4,32,768]{1,0,2:T(4,128)(2,1)S(1)} all-gather(bf16[4,32,192]{1,0,2:T(4,128)(2,1)S(1)} %copy.73), channel_id=1, replica_groups=mesh['groups'=2,'pairs'=4,'mp'=4] {'mp'}, dimensions={2}, use_global_device_ids=true | all-gather | bytes 245760 | tf_op jit(solution)/shard_map/all_gather | solution.py:72
  40.8 0.8 convert_reduce_fusion
  41.6 0.4 copy.74
  42.1 0.8 multiply_reduce_fusion.1
  42.9 0.7 div.88
  43.6 1.3 convert_element_type.84
  44.9 7.5 %rev.4 = f32[2,2,32,768]{2,1,0,3:T(2,128)S(1)} reverse(f32[2,2,32,768]{2,1,0,3:T(2,128)} %bitcast.83), dimensions={1} | reverse | bytes 786432 | tf_op jit(solution)/shard_map/jit(_flip)/rev | solution.py:34
  52.4 0.8 reduce_sum.93
  53.2 1.1 multiply_reduce_fusion
  54.4 0.6 copy.83
  55.2 0.8 fusion.18
  56.0 1.6 fusion.122
  57.6 0.1 reshape.312
  57.7 0.1 reshape.313
  57.9 0.2 convolution_multiply_fusion.1
  58.2 0.1 reshape.311
  58.4 0.3 fusion.6
  58.6 0.1 copy.82
  58.7 0.1 reshape.279
  58.9 0.9 convolution_convert_fusion.3
  59.9 0.1 fusion.15
  60.1 0.3 fusion.123
  60.5 0.1 reshape.316
  60.6 0.1 reshape.314
  60.7 28.6 %all-reduce.4.cloned.1.call-done = bf16[128,768]{1,0:T(8,128)(2,1)} async-done(((bf16[128,768]{1,0:T(8,128)(2,1)}), bf16[128,768]{1,0:T(8,128)(2,1)}) %all-reduce.4.cloned.1.call-update) | async-done | bytes 196624 | tf_op jit(solution)/shard_map/psum | solution.py:38
  89.3 1.0 fusion.77
  90.4 1.1 multiply_reduce_fusion.3
  91.5 0.3 convolution_convert_fusion.6
  91.8 0.1 reshape.315
  92.0 0.2 convolution_multiply_fusion
  92.3 0.3 fusion.7
  92.7 0.1 reshape.283
  92.8 0.9 convolution_convert_fusion.2
  93.9 31.7 %all-reduce.6.cloned.1.call-done = bf16[128,768]{1,0:T(8,128)(2,1)} async-done(((bf16[128,768]{1,0:T(8,128)(2,1)}), bf16[128,768]{1,0:T(8,128)(2,1)}) %all-reduce.6.cloned.1.call-update) | async-done | bytes 196624 | tf_op jit(solution)/shard_map/psum | solution.py:38
  125.6 1.1 fusion.117
  126.7 0.2 multiply_reduce_fusion.2
  126.9 2.1 %convolution_convert_fusion.1 = bf16[128,768]{1,0:T(8,128)(2,1)} fusion(bf16[768,768]{1,0:T(8,128)(2,1)S(1)} %copy-done, bf16[768,768]{1,0:T(8,128)(2,1)S(1)} %copy-done.13, f32[128,768]{1,0:T(8,128)S(1)} %get-tuple-element.6, f32[768]{0:T(1024)S(1)} %copy-done.14, f32[128]{0:T(128)S(1)} %add_rsqrt_fusion.2, f32[128]{0:T(128)S(1)} %broadcast_multiply_fusion.2), kind=kOutput, calls=%fused_computation.9 | convolution fusion | flops 308871168 | bytes 2953216 | tf_op jit(solution)/shard_map/dot_general | solution.py:99
  129.1 0.1 fusion.9
  129.2 0.6 copy.94
  129.8 4.6 %all-to-all-start.2 = ((bf16[4,1,32]{2,1,0:T(2,128)(2,1)}), bf16[4,1,32]{2,1,0:T(2,128)(2,1)S(1)}, u32[]{:S(2)}, u32[]{:S(2)}) async-start(bf16[4,1,32]{2,1,0:T(2,128)(2,1)} %copy.94), calls=%async_computation.2 | async-start | bytes 4096 | tf_op jit(solution)/shard_map/all_to_all | solution.py:113
  134.5 0.1 mul.147
  134.6 26.3 %all-reduce.8.cloned.1.call-done = bf16[128,768]{1,0:T(8,128)(2,1)} async-done(((bf16[128,768]{1,0:T(8,128)(2,1)}), bf16[128,768]{1,0:T(8,128)(2,1)}) %all-reduce.8.cloned.1.call-update) | async-done | bytes 196624 | tf_op jit(solution)/shard_map/psum | solution.py:38
  160.9 1.0 dynamic-slice_add_fusion
  161.9 0.1 reshape.284
  162.1 0.2 convolution_convert_fusion
  162.3 0.7 reshape.285
  163.0 4.6 %all-to-all-start.1 = ((bf16[4,32,192]{2,1,0:T(8,128)(2,1)}), bf16[4,32,192]{2,1,0:T(8,128)(2,1)S(1)}, u32[]{:S(2)}, u32[]{:S(2)}) async-start(bf16[4,32,192]{2,1,0:T(8,128)(2,1)} %reshape.285), calls=%async_computation.1 | async-start | bytes 131072 | tf_op jit(solution)/shard_map/all_to_all | solution.py:110
  167.6 0.1 convolution_maximum_fusion
  167.7 0.1 copy.95
  167.8 5.5 %all-to-all-done.1 = bf16[4,32,192]{2,1,0:T(8,128)(2,1)S(1)} async-done(((bf16[4,32,192]{2,1,0:T(8,128)(2,1)}), bf16[4,32,192]{2,1,0:T(8,128)(2,1)S(1)}, u32[]{:S(2)}, u32[]{:S(2)}) %all-to-all-start.1) | async-done | bytes 49184 | tf_op jit(solution)/shard_map/all_to_all | solution.py:110
  173.4 0.2 fusion.8
  173.5 0.6 copy.96
  (65 shorter events, 1.3 us)
Async XLA Ops:
  6.5 120.3 %copy-start = (bf16[768,768]{1,0:T(8,128)(2,1)S(1)}, bf16[768,768]{1,0:T(8,128)(2,1)}, u32[]{:S(2)}) copy-start(bf16[768,768]{1,0:T(8,128)(2,1)} %param.27) | copy-start | bytes 3538948
  19.8 0.5 copy-start.11
  22.4 9.0 %all-to-all-start = ((bf16[4,32,192]{2,1,0:T(8,128)(2,1)}), bf16[4,32,192]{2,1,0:T(8,128)(2,1)S(1)}, u32[]{:S(2)}, u32[]{:S(2)}) async-start(bf16[4,32,192]{2,1,0:T(8,128)(2,1)} %select_select_fusion), calls=%async_computation | async-start | bytes 131072 | tf_op jit(solution)/shard_map/all_to_all | solution.py:69
  25.7 63.6 %all-reduce.4.cloned.1.call-start = ((), (), s32[]{:S(2)}) async-start(), calls=%async_computation.3 | async-start | bytes 393216 | tf_op jit(solution)/shard_map/psum | solution.py:38
  53.2 1.9 %copy-start.6 = (f32[768]{0:T(1024)S(1)}, f32[768]{0:T(1024)}, u32[]{:S(2)}) copy-start(f32[768]{0:T(1024)} %param.17) | copy-start | bytes 9220
  57.6 1.3 copy-start.3
  57.9 2.0 %copy-start.7 = (f32[768]{0:T(1024)S(1)}, f32[768]{0:T(1024)}, u32[]{:S(2)}) copy-start(f32[768]{0:T(1024)} %param.19) | copy-start | bytes 9220
  58.2 1.9 %copy-start.2 = (bf16[2,768,192]{1,2,0:T(8,128)(2,1)S(1)}, bf16[2,768,192]{1,2,0:T(8,128)(2,1)}, u32[]{:S(2)}) copy-start(bf16[2,768,192]{1,2,0:T(8,128)(2,1)} %param.24) | copy-start | bytes 1769476
  59.8 65.8 %all-reduce.6.cloned.1.call-start = ((), (), s32[]{:S(2)}) async-start(), calls=%async_computation.4 | async-start | bytes 393216 | tf_op jit(solution)/shard_map/psum | solution.py:38
  60.1 31.4 %copy-start.4 = (bf16[768,192]{0,1:T(8,128)(2,1)S(1)}, bf16[768,192]{0,1:T(8,128)(2,1)}, u32[]{:S(2)}) copy-start(bf16[768,192]{0,1:T(8,128)(2,1)} %param.23) | copy-start | bytes 884740
  60.1 31.4 %copy-start.8 = (f32[768]{0:T(1024)S(1)}, f32[768]{0:T(1024)}, u32[]{:S(2)}) copy-start(f32[768]{0:T(1024)} %param.18) | copy-start | bytes 9220
  91.5 1.3 copy-start.5
  92.0 1.8 copy-start.9
  92.0 33.6 %copy-start.1 = (bf16[128,768]{1,0:T(8,128)(2,1)S(1)}, bf16[128,768]{1,0:T(8,128)(2,1)}, u32[]{:S(2)}) copy-start(bf16[128,768]{1,0:T(8,128)(2,1)} %all-reduce.4.cloned.1.call-done) | copy-start | bytes 589828
  92.6 34.3 %copy-start.14 = (f32[768]{0:T(1024)S(1)}, f32[768]{0:T(1024)}, u32[]{:S(2)}) copy-start(f32[768]{0:T(1024)} %param.20) | copy-start | bytes 9220
  93.7 67.2 %all-reduce.8.cloned.1.call-start = ((), (), s32[]{:S(2)}) async-start(), calls=%async_computation.5 | async-start | bytes 393216 | tf_op jit(solution)/shard_map/psum | solution.py:38
  93.9 33.0 %copy-start.13 = (bf16[768,768]{1,0:T(8,128)(2,1)S(1)}, bf16[768,768]{1,0:T(8,128)(2,1)}, u32[]{:S(2)}) copy-start(bf16[768,768]{1,0:T(8,128)(2,1)} %param.26) | copy-start | bytes 3538948
  126.9 2.2 %copy-start.10 = (s32[4]{0:T(128)S(1)}, s32[4]{0:T(128)}, u32[]{:S(2)}) copy-start(s32[4]{0:T(128)} %get-tuple-element.8) | copy-start | bytes 52
  129.1 38.6 %copy-start.12 = (s32[4]{0:T(128)S(1)}, s32[4]{0:T(128)}, u32[]{:S(2)}) copy-start(s32[4]{0:T(128)} %copy-done.11) | copy-start | bytes 52
  129.8 33.2 %all-to-all-start.2 = ((bf16[4,1,32]{2,1,0:T(2,128)(2,1)}), bf16[4,1,32]{2,1,0:T(2,128)(2,1)S(1)}, u32[]{:S(2)}, u32[]{:S(2)}) async-start(bf16[4,1,32]{2,1,0:T(2,128)(2,1)} %copy.94), calls=%async_computation.2 | async-start | bytes 4096 | tf_op jit(solution)/shard_map/all_to_all | solution.py:113
  163.0 10.3 %all-to-all-start.1 = ((bf16[4,32,192]{2,1,0:T(8,128)(2,1)}), bf16[4,32,192]{2,1,0:T(8,128)(2,1)S(1)}, u32[]{:S(2)}, u32[]{:S(2)}) async-start(bf16[4,32,192]{2,1,0:T(8,128)(2,1)} %reshape.285), calls=%async_computation.1 | async-start | bytes 131072 | tf_op jit(solution)/shard_map/all_to_all | solution.py:110
Sparse Core Ops, SparseCore 0:
  59.9 29.3 all-reduce.3
  93.8 31.7 all-reduce.5
  129.2 31.6 all-reduce.7
where the time goes:
time: 181 us
  waiting for transfers between devices  95.8 us (53%)
  blocking collectives  21.6 us (12%)
  local copies, waits for them, and re-layouts  17.5 us (10%)
  between operations  13.6 us (8%)
  starting transfers between devices  12.6 us (7%)
  other arithmetic  12 us (7%)
  matrix products  7.72 us (4%)
    psum x3, waiting for transfers between devices, summed_full(): return lax.psum(term.astype(jnp.bfloat16), 'mp').astype(jnp.float32)  86.6 us
    all_gather x1, blocking collectives, per_device(): lax.all_gather(pair_list, 'pairs', axis=0, tiled=True)  13 us
    all_gather x1, blocking collectives, per_device(): start = lax.all_gather(slices, 'mp', axis=2, tiled=True)  8.6 us
    rev x2, local copies, waits for them, and re-layouts, partner(): return jnp.flip(paired, axis=1).reshape(shape)  8.14 us
    all_to_all x1, waiting for transfers between devices, per_device(): lax.all_to_all(back.reshape(owners_n, TOKS, quarter), 'pairs', split_axis...  5.53 us
    all_to_all x1, starting transfers between devices, per_device(): lax.all_to_all(back_weight, 'pairs', split_axis=0, concat_axis=0, tiled=T...  4.6 us
    all_to_all x1, starting transfers between devices, per_device(): lax.all_to_all(back.reshape(owners_n, TOKS, quarter), 'pairs', split_axis...  4.6 us
    reduce_sum x4, other arithmetic, layer_norm(): center = values - jnp.mean(values, axis=-1, keepdims=True)  3.78 us
  transfers between devices with their start and end apart: 6, of which 5 were waited for; matrix products, arithmetic and copies ran while one was open for 3% of the time, Pallas kernels for 0%

commit v1 on v0

--- a/solution.py
+++ b/solution.py
@@ -69,7 +69,12 @@
     arrived = lax.all_to_all(outgoing, "pairs", split_axis=0, concat_axis=0, tiled=True)
     source = pair_list.reshape(views_n) // img_dev
     slices = jnp.take(arrived, source, axis=0)
-    start = lax.all_gather(slices, "mp", axis=2, tiled=True)
+    ring = [slices]
+    for hop in range(3):
+        ring.append(lax.ppermute(ring[-1], "mp", [(dev, (dev + 1) % 4) for dev in range(4)]))
+    start = jnp.roll(
+        jnp.concatenate(ring[::-1], axis=2), (lax.axis_index("mp") + 1) * ring[0].shape[2], axis=2
+    )
     width = start.shape[2]
     rows_n = views_n * TOKS
     begin = start.astype(jnp.float32).reshape(rows_n, width)

time: 181 us -> 173 us (0.956)
  waiting for transfers between devices: 95.8 us -> 109 us
  local copies, waits for them, and re-layouts: 17.5 us -> 8.31 us
  blocking collectives: 21.6 us -> 13 us
  other arithmetic: 12 us -> 8.13 us
    ppermute x0 -> x3, waiting for transfers between devices: none -> 11.1 us  [per_device(): lax.ppermute(ring[-1], 'mp', [(dev, (dev + 1) % 4) for dev in range(4)])]
    all_gather x1 -> x0, blocking collectives: 8.6 us -> none  [per_device(): start = lax.all_gather(slices, 'mp', axis=2, tiled=True)]
    rev x2 -> x1, local copies, waits for them, and re-layouts: 8.14 us -> 0.03 us  [partner(): return jnp.flip(paired, axis=1).reshape(shape)]
  transfers between devices with their start and end apart: 6 -> 9, of which waited for: 5 -> 8; matrix products, arithmetic and copies ran while one was open for 3% -> 3% of each run, Pallas kernels for 0% -> 0%
where the time goes in v1:
time: 173 us; the launch traced here: 172 us
  waiting for transfers between devices  109 us (63%)
  between operations  13.6 us (8%)
  blocking collectives  13 us (8%)
  starting transfers between devices  12.6 us (7%)
  local copies, waits for them, and re-layouts  8.31 us (5%)
  other arithmetic  8.13 us (5%)
  matrix products  7.72 us (4%)
    psum x3, waiting for transfers between devices, summed_full(): return lax.psum(term.astype(jnp.bfloat16), 'mp').astype(jnp.float32)  88.1 us
    all_gather x1, blocking collectives, per_device(): lax.all_gather(pair_list, 'pairs', axis=0, tiled=True)  13 us
    ppermute x3, waiting for transfers between devices, per_device(): lax.ppermute(ring[-1], 'mp', [(dev, (dev + 1) % 4) for dev in range(4)])  11.1 us
    all_to_all x1, waiting for transfers between devices, per_device(): lax.all_to_all(back.reshape(owners_n, TOKS, quarter), 'pairs', split_axis...  5.53 us
    all_to_all x1, starting transfers between devices, per_device(): lax.all_to_all(back.reshape(owners_n, TOKS, quarter), 'pairs', split_axis...  4.6 us
    all_to_all x1, starting transfers between devices, per_device(): lax.all_to_all(back_weight, 'pairs', split_axis=0, concat_axis=0, tiled=T...  4.6 us
    all_to_all x1, waiting for transfers between devices, per_device(): lax.all_to_all(outgoing, 'pairs', split_axis=0, concat_axis=0, tiled=True)  4.1 us
  transfers between devices with their start and end apart: 9, of which 8 were waited for; matrix products, arithmetic and copies ran while one was open for 3% of the time, Pallas kernels for 0%

profile of v1, /device:TPU:0, one launch (start us, length us, event | category | flops | bytes accessed | tf_op | source)
XLA Modules:
  0.0 172.2 jit_solution(10626616977184623155)
XLA Ops:
  6.5 13.0 %all-gather = s32[4,2,2]{2,1,0:T(2,128)S(1)} all-gather(s32[1,2,2]{2,1,0:T(2,128)} %bitcast.95), channel_id=1, replica_groups=mesh['groups'=2,'pairs'=4,'mp'=4] {'pairs'}, dimensions={0}, use_global_device_ids=true | all-gather | bytes 80 | tf_op jit(solution)/shard_map/all_gather | solution.py:63
  19.7 0.1 reduce_max.36
  19.9 1.3 gather_fusion
  21.2 0.7 select_select_fusion
  21.9 3.3 %all-to-all-start = ((bf16[4,32,192]{2,1,0:T(8,128)(2,1)}), bf16[4,32,192]{2,1,0:T(8,128)(2,1)S(1)}, u32[]{:S(2)}, u32[]{:S(2)}) async-start(bf16[4,32,192]{2,1,0:T(8,128)(2,1)} %select_select_fusion), calls=%async_computation | async-start | bytes 131072 | tf_op jit(solution)/shard_map/all_to_all | solution.py:69
  25.2 0.8 reshape.277
  26.0 0.8 reshape.275
  26.8 4.1 %all-to-all-done = bf16[4,32,192]{2,1,0:T(8,128)(2,1)S(1)} async-done(((bf16[4,32,192]{2,1,0:T(8,128)(2,1)}), bf16[4,32,192]{2,1,0:T(8,128)(2,1)S(1)}, u32[]{:S(2)}, u32[]{:S(2)}) %all-to-all-start) | async-done | bytes 49184 | tf_op jit(solution)/shard_map/all_to_all | solution.py:69
  30.9 0.5 gather_fusion.1
  31.5 3.7 %collective-permute-done = bf16[4,32,192]{2,1,0:T(8,128)(2,1)S(1)} collective-permute-done((bf16[4,32,192]{2,1,0:T(8,128)(2,1)S(1)}, bf16[4,32,192]{2,1,0:T(8,128)(2,1)S(1)}, u32[]{:S(2)}, u32[]{:S(2)}) %collective-permute-start) | collective-permute-done | bytes 49184 | tf_op jit(solution)/shard_map/ppermute | solution.py:74
  35.2 3.7 %collective-permute-done.1 = bf16[4,32,192]{2,1,0:T(8,128)(2,1)S(1)} collective-permute-done((bf16[4,32,192]{2,1,0:T(8,128)(2,1)S(1)}, bf16[4,32,192]{2,1,0:T(8,128)(2,1)S(1)}, u32[]{:S(2)}, u32[]{:S(2)}) %collective-permute-start.1) | collective-permute-done | bytes 49184 | tf_op jit(solution)/shard_map/ppermute | solution.py:74
  38.9 3.7 %collective-permute-done.2 = bf16[4,32,192]{2,1,0:T(8,128)(2,1)S(1)} collective-permute-done((bf16[4,32,192]{2,1,0:T(8,128)(2,1)S(1)}, bf16[4,32,192]{2,1,0:T(8,128)(2,1)S(1)}, u32[]{:S(2)}, u32[]{:S(2)}) %collective-permute-start.2) | collective-permute-done | bytes 49184 | tf_op jit(solution)/shard_map/ppermute | solution.py:74
  42.6 0.2 concatenate.6
  42.8 0.1 dynamic-slice_convert_fusion
  43.0 0.1 reverse_reduce_fusion
  43.1 0.2 multiply_reduce_fusion.2
  43.4 0.2 convert_reduce_fusion
  43.6 0.2 multiply_reduce_fusion.3
  44.0 0.1 fusion.15
  44.2 0.3 fusion.120
  44.6 0.2 fusion.18
  44.8 0.3 copy-done.2
  45.1 0.4 fusion.119
  45.5 0.1 reshape.311
  45.6 0.1 reshape.313
  45.8 0.1 reshape.312
  45.9 0.2 convolution_multiply_fusion.1
  46.2 0.3 fusion.6
  46.5 0.1 copy.78
  46.6 0.1 reshape.279
  46.8 0.1 copy-done.4
  46.9 0.9 convolution_convert_fusion.3
  47.9 0.1 reshape.314
  48.0 0.1 reshape.316
  48.1 30.1 %all-reduce.4.cloned.1.call-done = bf16[128,768]{1,0:T(8,128)(2,1)} async-done(((bf16[128,768]{1,0:T(8,128)(2,1)}), bf16[128,768]{1,0:T(8,128)(2,1)}) %all-reduce.4.cloned.1.call-update) | async-done | bytes 196624 | tf_op jit(solution)/shard_map/psum | solution.py:38
  78.2 1.1 fusion.26
  79.3 1.2 multiply_reduce_fusion.1
  80.5 1.1 multiply_convert_fusion.1
  81.7 0.2 convolution_convert_fusion.6
  81.9 0.1 reshape.315
  82.1 0.2 convolution_multiply_fusion
  82.4 0.3 fusion.7
  82.8 0.1 reshape.283
  82.9 0.1 copy-done.6
  83.0 0.9 convolution_convert_fusion.2
  84.1 31.7 %all-reduce.6.cloned.1.call-done = bf16[128,768]{1,0:T(8,128)(2,1)} async-done(((bf16[128,768]{1,0:T(8,128)(2,1)}), bf16[128,768]{1,0:T(8,128)(2,1)}) %all-reduce.6.cloned.1.call-update) | async-done | bytes 196624 | tf_op jit(solution)/shard_map/psum | solution.py:38
  115.8 1.1 fusion.114
  117.0 0.2 multiply_reduce_fusion
  117.2 3.4 %convolution_convert_fusion.1 = bf16[128,768]{1,0:T(8,128)(2,1)} fusion(bf16[768,768]{1,0:T(8,128)(2,1)S(1)} %copy-done, bf16[768,768]{1,0:T(8,128)(2,1)} %param.26, f32[128,768]{1,0:T(8,128)S(1)} %get-tuple-element.6, f32[768]{0:T(1024)S(1)} %copy-done.11, f32[128]{0:T(128)S(1)} %add_rsqrt_fusion.2, f32[128]{0:T(128)S(1)} %broadcast_multiply_fusion.2), kind=kOutput, calls=%fused_computation.7 | convolution fusion | flops 308871168 | bytes 2953216 | tf_op jit(solution)/shard_map/dot_general | solution.py:104
  120.6 0.1 fusion.9
  120.7 0.6 copy.89
  121.3 4.6 %all-to-all-start.2 = ((bf16[4,1,32]{2,1,0:T(2,128)(2,1)}), bf16[4,1,32]{2,1,0:T(2,128)(2,1)S(1)}, u32[]{:S(2)}, u32[]{:S(2)}) async-start(bf16[4,1,32]{2,1,0:T(2,128)(2,1)} %copy.89), calls=%async_computation.2 | async-start | bytes 4096 | tf_op jit(solution)/shard_map/all_to_all | solution.py:118
  126.0 0.1 mul.151
  126.1 26.3 %all-reduce.8.cloned.1.call-done = bf16[128,768]{1,0:T(8,128)(2,1)} async-done(((bf16[128,768]{1,0:T(8,128)(2,1)}), bf16[128,768]{1,0:T(8,128)(2,1)}) %all-reduce.8.cloned.1.call-update) | async-done | bytes 196624 | tf_op jit(solution)/shard_map/psum | solution.py:38
  152.5 1.0 dynamic-slice_add_fusion
  153.5 0.1 reshape.284
  153.6 0.2 convolution_convert_fusion
  153.8 0.7 reshape.285
  154.6 4.6 %all-to-all-start.1 = ((bf16[4,32,192]{2,1,0:T(8,128)(2,1)}), bf16[4,32,192]{2,1,0:T(8,128)(2,1)S(1)}, u32[]{:S(2)}, u32[]{:S(2)}) async-start(bf16[4,32,192]{2,1,0:T(8,128)(2,1)} %reshape.285), calls=%async_computation.1 | async-start | bytes 131072 | tf_op jit(solution)/shard_map/all_to_all | solution.py:115
  159.2 0.1 convolution_maximum_fusion
  159.3 0.1 copy.90
  159.4 5.5 %all-to-all-done.1 = bf16[4,32,192]{2,1,0:T(8,128)(2,1)S(1)} async-done(((bf16[4,32,192]{2,1,0:T(8,128)(2,1)}), bf16[4,32,192]{2,1,0:T(8,128)(2,1)S(1)}, u32[]{:S(2)}, u32[]{:S(2)}) %all-to-all-start.1) | async-done | bytes 49184 | tf_op jit(solution)/shard_map/all_to_all | solution.py:115
  164.9 0.2 fusion.8
  165.1 0.6 copy.91
  (63 shorter events, 1.4 us)
Async XLA Ops:
  6.5 110.6 %copy-start = (bf16[768,768]{1,0:T(8,128)(2,1)S(1)}, bf16[768,768]{1,0:T(8,128)(2,1)}, u32[]{:S(2)}) copy-start(bf16[768,768]{1,0:T(8,128)(2,1)} %param.27) | copy-start | bytes 3538948
  21.9 9.0 %all-to-all-start = ((bf16[4,32,192]{2,1,0:T(8,128)(2,1)}), bf16[4,32,192]{2,1,0:T(8,128)(2,1)S(1)}, u32[]{:S(2)}, u32[]{:S(2)}) async-start(bf16[4,32,192]{2,1,0:T(8,128)(2,1)} %select_select_fusion), calls=%async_computation | async-start | bytes 131072 | tf_op jit(solution)/shard_map/all_to_all | solution.py:69
  25.2 53.0 %all-reduce.4.cloned.1.call-start = ((), (), s32[]{:S(2)}) async-start(), calls=%async_computation.3 | async-start | bytes 393216 | tf_op jit(solution)/shard_map/psum | solution.py:38
  31.5 3.7 %collective-permute-start = (bf16[4,32,192]{2,1,0:T(8,128)(2,1)S(1)}, bf16[4,32,192]{2,1,0:T(8,128)(2,1)S(1)}, u32[]{:S(2)}, u32[]{:S(2)}) collective-permute-start(bf16[4,32,192]{2,1,0:T(8,128)(2,1)S(1)} %broadcast_select_fusion), channel_id=1, source_target_pairs={{0,1},{1,2},{2,3},{3,0},{4,5},{5,6},{6,7},{7,4},{8,9},{9,10},{10,1... | collective-permute-start | bytes 147464 | tf_op jit(solution)/shard_map/ppermute | solution.py:74
  35.2 3.7 %collective-permute-start.1 = (bf16[4,32,192]{2,1,0:T(8,128)(2,1)S(1)}, bf16[4,32,192]{2,1,0:T(8,128)(2,1)S(1)}, u32[]{:S(2)}, u32[]{:S(2)}) collective-permute-start(bf16[4,32,192]{2,1,0:T(8,128)(2,1)S(1)} %collective-permute-done), channel_id=1, source_target_pairs={{0,1},{1,2},{2,3},{3,0},{4,5},{5,6},{6,7},{7,4},{8,9},{9,10},{10,1... | collective-permute-start | bytes 147464 | tf_op jit(solution)/shard_map/ppermute | solution.py:74
  38.9 3.7 %collective-permute-start.2 = (bf16[4,32,192]{2,1,0:T(8,128)(2,1)S(1)}, bf16[4,32,192]{2,1,0:T(8,128)(2,1)S(1)}, u32[]{:S(2)}, u32[]{:S(2)}) collective-permute-start(bf16[4,32,192]{2,1,0:T(8,128)(2,1)S(1)} %collective-permute-done.1), channel_id=1, source_target_pairs={{0,1},{1,2},{2,3},{3,0},{4,5},{5,6},{6,7},{7,4},{8,9},{9,10},{10,1... | collective-permute-start | bytes 147464 | tf_op jit(solution)/shard_map/ppermute | solution.py:74
  42.8 1.3 copy-start.7
  42.9 1.2 copy-start.3
  43.3 1.3 copy-start.8
  43.9 1.2 copy-start.2
  45.9 1.0 copy-start.4
  46.6 33.9 %copy-start.9 = (f32[768]{0:T(1024)S(1)}, f32[768]{0:T(1024)}, u32[]{:S(2)}) copy-start(f32[768]{0:T(1024)} %param.18) | copy-start | bytes 9220
  47.8 33.9 %copy-start.5 = (bf16[768,192]{0,1:T(8,128)(2,1)S(1)}, bf16[768,192]{0,1:T(8,128)(2,1)}, u32[]{:S(2)}) copy-start(bf16[768,192]{0,1:T(8,128)(2,1)} %param.23) | copy-start | bytes 884740
  47.8 68.0 %all-reduce.6.cloned.1.call-start = ((), (), s32[]{:S(2)}) async-start(), calls=%async_computation.4 | async-start | bytes 393216 | tf_op jit(solution)/shard_map/psum | solution.py:38
  82.1 1.0 copy-start.6
  82.4 1.6 copy-start.10
  82.4 33.4 %copy-start.1 = (bf16[128,768]{1,0:T(8,128)(2,1)S(1)}, bf16[128,768]{1,0:T(8,128)(2,1)}, u32[]{:S(2)}) copy-start(bf16[128,768]{1,0:T(8,128)(2,1)} %all-reduce.4.cloned.1.call-done) | copy-start | bytes 589828
  82.8 34.4 %copy-start.11 = (f32[768]{0:T(1024)S(1)}, f32[768]{0:T(1024)}, u32[]{:S(2)}) copy-start(f32[768]{0:T(1024)} %param.20) | copy-start | bytes 9220
  83.9 68.5 %all-reduce.8.cloned.1.call-start = ((), (), s32[]{:S(2)}) async-start(), calls=%async_computation.5 | async-start | bytes 393216 | tf_op jit(solution)/shard_map/psum | solution.py:38
  121.3 33.2 %all-to-all-start.2 = ((bf16[4,1,32]{2,1,0:T(2,128)(2,1)}), bf16[4,1,32]{2,1,0:T(2,128)(2,1)S(1)}, u32[]{:S(2)}, u32[]{:S(2)}) async-start(bf16[4,1,32]{2,1,0:T(2,128)(2,1)} %copy.89), calls=%async_computation.2 | async-start | bytes 4096 | tf_op jit(solution)/shard_map/all_to_all | solution.py:118
  154.6 10.3 %all-to-all-start.1 = ((bf16[4,32,192]{2,1,0:T(8,128)(2,1)}), bf16[4,32,192]{2,1,0:T(8,128)(2,1)S(1)}, u32[]{:S(2)}, u32[]{:S(2)}) async-start(bf16[4,32,192]{2,1,0:T(8,128)(2,1)} %reshape.285), calls=%async_computation.1 | async-start | bytes 131072 | tf_op jit(solution)/shard_map/all_to_all | solution.py:115
Sparse Core Ops, SparseCore 0:
  47.9 30.2 all-reduce.3
  84.0 31.7 all-reduce.5
  120.7 31.6 all-reduce.7
